TPU v7x, 32 devices: a whole 2x2x4 slice. The times are simulated.
32 devices in a mesh: freq: 2 (over x), row: 4 (over z), col: 4 (over y, core).
Axes of the slice: x: 2, y: 2, z: 4, core: 2. Of those that a mesh axis runs over, the one named last changes fastest.
Arguments:
- sky_maps: bfloat16 [512, 128, 512], P('freq', 'row', 'col'), may hold values from -32 to 32
- beam_sigma: float32 [512], P('freq'), may hold values from 1.5 to 4
- whitening: bfloat16 [512, 512], replicated, may hold values from -0.25 to 0.25
- unmix_init: float32 [128, 512], replicated, may hold values from -0.25 to 0.25
Outputs:
- unmixing: float32 [128, 512], replicated
- sources: bfloat16 [128, 65536], P(None, ('freq', 'row', 'col'))
All inputs are finite; a program needn't handle non-finite values.
Results may differ from a plain program's by a relative error of at most 0.0025.
The roundings to bfloat16 on the way count: a program that leaves them out, or rounds other values in their place, can miss the bound.
Values may be sent and summed in bfloat16 or wider, within the bound.
No kernel may reach another device: no remote copies, remote signals or barrier semaphores. Data moves between devices by JAX's collectives and lax.ppermute only.
A program may use at most 64 MiB of HBM per device.

v0:
```python
import jax
import jax.numpy as jnp
from jax import lax
from jax.sharding import PartitionSpec as P

HALF = 8
ITERS = 2
NS_STEPS = 5


def with_halo(cells, sides, width):
    for axis, dim in sides:
        count = lax.axis_size(axis)
        ends = count - 1
        head = lax.slice_in_dim(cells, 0, width, axis=dim)
        tail = lax.slice_in_dim(cells, cells.shape[dim] - width, cells.shape[dim], axis=dim)
        cells = jnp.concatenate(
            [
                lax.ppermute(tail, axis, [(i, (i + 1) % count) for i in range(ends)]),
                cells,
                lax.ppermute(head, axis, [((i + 1) % count, i) for i in range(ends)]),
            ],
            axis=dim,
        )
    return cells


def make_taps(beam_sigma):
    offsets = jnp.arange(2 * HALF + 1, dtype=jnp.float32) - HALF
    shaped = jnp.exp(
        -(offsets[None, :] * offsets[None, :]) / (2.0 * beam_sigma[:, None] * beam_sigma[:, None])
    )
    return (shaped / jnp.sum(shaped, axis=1, keepdims=True)).astype(jnp.bfloat16)


def make_band(beam_taps, length):
    spread = beam_taps.shape[1]
    offsets = jnp.arange(length + spread - 1)[None, :] - jnp.arange(length)[:, None]
    onehot = (offsets[:, :, None] == jnp.arange(spread)[None, None, :]).astype(jnp.float32)
    return jnp.einsum("ijk,ck->cij", onehot, beam_taps.astype(jnp.float32)).astype(jnp.bfloat16)


def inverse_root(matrix):
    frob_norm = jnp.sqrt(jnp.sum(matrix * matrix) + 1e-06)
    current = matrix / frob_norm
    unit_matrix = jnp.eye(matrix.shape[0], dtype=jnp.float32)
    inverse = unit_matrix
    for iteration in range(NS_STEPS):
        correction = 0.5 * (
            3.0 * unit_matrix - jnp.dot(inverse, current, precision=lax.Precision.HIGHEST)
        )
        current = jnp.dot(current, correction, precision=lax.Precision.HIGHEST)
        inverse = jnp.dot(correction, inverse, precision=lax.Precision.HIGHEST)
    return inverse / jnp.sqrt(frob_norm)


def pixel_moments(coarse, whitened):
    outputs = jnp.dot(coarse, whitened, preferred_element_type=jnp.float32)
    cubed = (outputs * outputs * outputs).astype(jnp.bfloat16)
    return lax.dot_general(
        cubed, whitened, (((1,), (1,)), ((), ())), preferred_element_type=jnp.float32
    )


def shards(sky_maps, beam_sigma, whitening, unmix_init):
    beam_taps = make_taps(beam_sigma)
    channels, height, breadth = sky_maps.shape
    band_rows = make_band(beam_taps, height)
    band_cols = make_band(beam_taps, breadth)
    padded = with_halo(sky_maps, (("row", 1),), HALF)
    rowwise = jnp.einsum(
        "cik,ckj->cij", band_rows, padded, preferred_element_type=jnp.float32
    ).astype(jnp.bfloat16)
    widened = with_halo(rowwise, (("col", 2),), HALF)
    smoothed = jnp.einsum(
        "cim,cjm->cij", widened, band_cols, preferred_element_type=jnp.float32
    ).astype(jnp.bfloat16)
    plane_sums = lax.psum(jnp.sum(smoothed, axis=(1, 2), dtype=jnp.float32), ("row", "col"))
    flattened = smoothed.reshape(channels, height * breadth)
    spectra = lax.all_to_all(flattened, "freq", split_axis=1, concat_axis=0, tiled=True)
    devices = lax.axis_size("freq") * lax.axis_size("row") * lax.axis_size("col")
    total_pixels = spectra.shape[1] * devices
    channel_sums = lax.all_gather(plane_sums, "freq", axis=0, tiled=True)
    means = channel_sums / total_pixels
    shift = jnp.dot(whitening.astype(jnp.float32), means, precision=lax.Precision.HIGHEST)
    whitened = (
        jnp.dot(whitening, spectra, preferred_element_type=jnp.float32) - shift[:, None]
    ).astype(jnp.bfloat16)
    unmixing = unmix_init
    for iteration in range(ITERS):
        moments = pixel_moments(unmixing.astype(jnp.bfloat16), whitened)
        moments = lax.psum(moments, ("freq", "row", "col"))
        updated = moments / total_pixels - 3.0 * unmixing
        gram = jnp.dot(updated, updated.T, precision=lax.Precision.HIGHEST)
        unmixing = jnp.dot(inverse_root(gram), updated, precision=lax.Precision.HIGHEST)
    sources = jnp.dot(
        unmixing.astype(jnp.bfloat16), whitened, preferred_element_type=jnp.float32
    ).astype(jnp.bfloat16)
    return (unmixing, sources)


def solution(mesh):
    return jax.shard_map(
        shards,
        mesh=mesh,
        in_specs=(P("freq", "row", "col"), P("freq"), P(), P()),
        out_specs=(P(), P(None, ("freq", "row", "col"))),
        check_vma=False,
    )
```

profile of v0, /device:TPU:0, one launch (start us, length us, event | category | flops | bytes accessed | tf_op | source)
XLA Modules:
  0.0 394.4 jit_solution(6294452238984527691)
XLA Ops:
  8.5 5.0 %collective-permute-start = (bf16[256,8,128]{2,1,0:T(8,128)(2,1)S(1)}, bf16[256,8,128]{2,1,0:T(8,128)(2,1)S(1)}, u32[]{:S(2)}, u32[]{:S(2)}) collective-permute-start(bf16[256,8,128]{2,1,0:T(8,128)(2,1)S(1)} %get-tuple-element.4), channel_id=1, source_target_pairs={{0,4},{4,8},{8,12},{1,5},{5,9},{9,13},{2,6},{6,10},{10,14},{3,7},{... | collective-permute-start | bytes 1572872 | tf_op jit(solution)/shard_map/ppermute | solution.py:19
  15.4 3.8 copy.7
  19.2 5.4 %collective-permute-done = bf16[256,8,128]{2,1,0:T(8,128)(2,1)S(1)} collective-permute-done((bf16[256,8,128]{2,1,0:T(8,128)(2,1)S(1)}, bf16[256,8,128]{2,1,0:T(8,128)(2,1)S(1)}, u32[]{:S(2)}, u32[]{:S(2)}) %collective-permute-start) | collective-permute-done | bytes 524320 | tf_op jit(solution)/shard_map/ppermute | solution.py:19
  24.6 4.3 %collective-permute-done.1 = bf16[256,8,128]{2,1,0:T(8,128)(2,1)} collective-permute-done((bf16[256,8,128]{2,1,0:T(8,128)(2,1)S(1)}, bf16[256,8,128]{2,1,0:T(8,128)(2,1)}, u32[]{:S(2)}, u32[]{:S(2)}) %collective-permute-start.1) | collective-permute-done | bytes 524320 | tf_op jit(solution)/shard_map/ppermute | solution.py:21
  28.9 3.3 fusion.13
  32.2 2.9 fusion.75
  35.1 2.7 copy.8
  37.8 2.7 copy.9
  41.8 3.0 collective-permute-start.2
  44.9 5.2 %convolution_convert_fusion = bf16[256,128,144]{1,0,2:T(8,128)(2,1)} fusion(s32[128,144]{0,1:T(8,128)S(1)} %iota_subtract_fusion, f32[256]{0:T(256)S(1)} %fusion.55, f32[256]{0:T(256)S(1)} %multiply_multiply_fusion.2, f32[17]{0:T(128)S(1)} %multiply_negate_fusion), kind=kOutput, calls=%fused_computation.2 | convolution fusion | flops 165477120 | bytes 9513028 | tf_op jit(solution)/shard_map/ijk,ck->cij/dot_general | solution.py:40
  50.1 3.7 copy.10
  53.8 3.7 copy.11
  57.5 17.0 %convert_reduce_fusion = (f32[256]{0:T(256)S(1)}, bf16[256,32,128]{2,1,0:T(8,128)(2,1)}) fusion(bf16[256,128,144]{1,0,2:T(8,128)(2,1)} %convolution_convert_fusion, bf16[256,32,8]{2,1,0:T(8,128)(2,1)} %copy.11, bf16[256,32,128]{2,1,0:T(8,128)(2,1)S(1)} %fusion.13, bf16[256,32,8]{2,1,0:T(8,128)(2,1)} %copy.10), kind=kOutput, calls=%fused_computation.9 | convolution fusion | flops 312213248 | bytes 13894656 | tf_op jit(solution)/shard_map/cim,cjm->cij/dot_general | solution.py:75
  74.4 2.5 all_to_all.14
  77.0 2.2 copy.13
  79.2 3.8 all-to-all-start
  83.0 30.9 %psum.21 = f32[256]{0:T(256)S(1)} all-reduce(f32[256]{0:T(256)S(1)} %get-tuple-element.6), channel_id=1, replica_groups=mesh['freq'=2,'row'=4,'col'=4] {'row','col'}, use_global_device_ids=true, to_apply=%region_2.0 | all-reduce | flops 256 | bytes 2048 | tf_op jit(solution)/shard_map/psum | solution.py:78
  113.9 4.5 %all-gather = f32[2,1,256]{2,1,0:T(1,128)S(1)} all-gather(f32[1,1,256]{2,1,0:T(1,128)S(1)} %bitcast.82), channel_id=1, replica_groups=mesh['freq'=2,'row'=4,'col'=4] {'freq'}, dimensions={0}, use_global_device_ids=true | all-gather | bytes 3072 | tf_op jit(solution)/shard_map/all_gather | solution.py:83
  120.2 2.9 subtract_convert_fusion
  123.2 1.9 fusion.22
  125.1 122.5 %all-reduce.3.cloned.1.call-done = f32[128,512]{1,0:T(8,128)} async-done(((f32[128,512]{1,0:T(8,128)}), f32[128,512]{1,0:T(8,128)}) %all-reduce.3.cloned.1.call-update) | async-done | bytes 262160 | tf_op jit(solution)/shard_map/psum | solution.py:92
  247.6 2.1 multiply_reduce_fusion.1
  255.6 124.1 %all-reduce.5.cloned.1.call-done = f32[128,512]{1,0:T(8,128)} async-done(((f32[128,512]{1,0:T(8,128)}), f32[128,512]{1,0:T(8,128)}) %all-reduce.5.cloned.1.call-update) | async-done | bytes 262160 | tf_op jit(solution)/shard_map/psum | solution.py:92
  379.7 2.1 multiply_reduce_fusion
  (64 shorter events, 16.3 us)
Async XLA Ops:
  7.2 111.2 %copy-start = (bf16[512,512]{1,0:T(8,128)(2,1)S(1)}, bf16[512,512]{1,0:T(8,128)(2,1)}, u32[]{:S(2)}) copy-start(bf16[512,512]{1,0:T(8,128)(2,1)} %param.6) | copy-start | bytes 1572868
  7.2 7.6 %copy-start.6 = (f32[256]{0:T(256)S(1)}, f32[256]{0:T(256)}, u32[]{:S(2)}) copy-start(f32[256]{0:T(256)} %param.5) | copy-start | bytes 3076
  8.5 16.1 %collective-permute-start = (bf16[256,8,128]{2,1,0:T(8,128)(2,1)S(1)}, bf16[256,8,128]{2,1,0:T(8,128)(2,1)S(1)}, u32[]{:S(2)}, u32[]{:S(2)}) collective-permute-start(bf16[256,8,128]{2,1,0:T(8,128)(2,1)S(1)} %get-tuple-element.4), channel_id=1, source_target_pairs={{0,4},{4,8},{8,12},{1,5},{5,9},{9,13},{2,6},{6,10},{10,14},{3,7},{... | collective-permute-start | bytes 1572872 | tf_op jit(solution)/shard_map/ppermute | solution.py:19
  13.5 15.4 %collective-permute-start.1 = (bf16[256,8,128]{2,1,0:T(8,128)(2,1)S(1)}, bf16[256,8,128]{2,1,0:T(8,128)(2,1)}, u32[]{:S(2)}, u32[]{:S(2)}) collective-permute-start(bf16[256,8,128]{2,1,0:T(8,128)(2,1)S(1)} %get-tuple-element.5), channel_id=1, source_target_pairs={{4,0},{8,4},{12,8},{5,1},{9,5},{13,9},{6,2},{10,6},{14,10},{7,3},{... | collective-permute-start | bytes 1572872 | tf_op jit(solution)/shard_map/ppermute | solution.py:21
  40.5 13.3 %collective-permute-start.3 = (bf16[256,32,8]{0,2,1:T(8,128)(2,1)S(1)}, bf16[256,32,8]{0,2,1:T(8,128)(2,1)S(1)}, u32[]{:S(2)}, u32[]{:S(2)}) collective-permute-start(bf16[256,32,8]{0,2,1:T(8,128)(2,1)S(1)} %copy.9), channel_id=1, source_target_pairs={{1,0},{2,1},{3,2},{5,4},{6,5},{7,6},{9,8},{10,9},{11,10},{13,12},{... | collective-permute-start | bytes 393224 | tf_op jit(solution)/shard_map/ppermute | solution.py:21
  41.8 8.2 %collective-permute-start.2 = (bf16[256,32,8]{0,2,1:T(8,128)(2,1)S(1)}, bf16[256,32,8]{0,2,1:T(8,128)(2,1)S(1)}, u32[]{:S(2)}, u32[]{:S(2)}) collective-permute-start(bf16[256,32,8]{0,2,1:T(8,128)(2,1)S(1)} %copy.8), channel_id=1, source_target_pairs={{0,1},{1,2},{2,3},{4,5},{5,6},{6,7},{8,9},{9,10},{10,11},{12,13},{... | collective-permute-start | bytes 393224 | tf_op jit(solution)/shard_map/ppermute | solution.py:19
  79.2 39.6 %all-to-all-start = ((bf16[256,2,2048]{2,0,1:T(8,128)(2,1)}), bf16[256,2,2048]{2,0,1:T(8,128)(2,1)S(1)}, u32[]{:S(2)}, u32[]{:S(2)}) async-start(bf16[256,2,2048]{2,0,1:T(8,128)(2,1)} %copy.13), calls=%async_computation | async-start | bytes 4194304 | tf_op jit(solution)/shard_map/all_to_all | solution.py:80
  83.0 164.6 %all-reduce.3.cloned.1.call-start = ((), (), s32[]{:S(2)}) async-start(), calls=%async_computation.1 | async-start | bytes 524288 | tf_op jit(solution)/shard_map/psum | solution.py:92
  118.8 1.4 copy-start.2
  120.2 3.0 copy-start.1
  125.1 254.7 %all-reduce.5.cloned.1.call-start = ((), (), s32[]{:S(2)}) async-start(), calls=%async_computation.2 | async-start | bytes 524288 | tf_op jit(solution)/shard_map/psum | solution.py:92
  247.6 5.8 %copy-start.3 = (f32[128,512]{1,0:T(8,128)S(1)}, f32[128,512]{1,0:T(8,128)}, u32[]{:S(2)}) copy-start(f32[128,512]{1,0:T(8,128)} %all-reduce.3.cloned.1.call-done) | copy-start | bytes 786436
  379.7 5.8 %copy-start.4 = (f32[128,512]{1,0:T(8,128)S(1)}, f32[128,512]{1,0:T(8,128)}, u32[]{:S(2)}) copy-start(f32[128,512]{1,0:T(8,128)} %all-reduce.5.cloned.1.call-done) | copy-start | bytes 786436
  385.9 1.6 copy-start.5
Sparse Core Ops, SparseCore 0:
  125.2 122.3 all-reduce.2
  255.7 123.9 all-reduce.4
where the time goes:
time: 395 us; the launch traced here: 394 us
  waiting for transfers between devices  256 us (65%)
  matrix products  45.3 us (11%)
  blocking collectives  35.3 us (9%)
  local copies, waits for them, and re-layouts  27 us (7%)
  between operations  15.9 us (4%)
  starting transfers between devices  14.4 us (4%)
    psum x2, waiting for transfers between devices, shards(): moments = lax.psum(moments, ('freq', 'row', 'col'))  247 us
    psum x1, blocking collectives, shards(): lax.psum(jnp.sum(smoothed, axis=(1, 2), dtype=jnp.float32), ('row', 'col'))  30.9 us
    dot_general x1, matrix products, shards(): jnp.einsum('cim,cjm->cij', widened, band_cols, preferred_element_type=jnp...  17 us
    ppermute x2, starting transfers between devices, with_halo(): lax.ppermute(tail, axis, [(i, (i + 1) % count) for i in range(ends)])  8 us
  transfers between devices with their start and end apart: 7, of which 4 were waited for; matrix products, arithmetic and copies ran while one was open for 3% of the time, Pallas kernels for 0%

commit v1 on v0

--- a/solution.py
+++ b/solution.py
@@ -89,7 +89,7 @@
     unmixing = unmix_init
     for iteration in range(ITERS):
         moments = pixel_moments(unmixing.astype(jnp.bfloat16), whitened)
-        moments = lax.psum(moments, ("freq", "row", "col"))
+        moments = lax.psum(lax.psum(moments, ("row", "col")), "freq")
         updated = moments / total_pixels - 3.0 * unmixing
         gram = jnp.dot(updated, updated.T, precision=lax.Precision.HIGHEST)
         unmixing = jnp.dot(inverse_root(gram), updated, precision=lax.Precision.HIGHEST)

time: 395 us -> 375 us (0.949)
  waiting for transfers between devices: 256 us -> 237 us
    psum x2 -> x4, waiting for transfers between devices: 247 us -> 227 us  [shards(): moments = lax.psum(lax.psum(moments, ('row', 'col')), 'freq')]
  transfers between devices with their start and end apart: 7 -> 9, of which waited for: 4 -> 6; matrix products, arithmetic and copies ran while one was open for 3% -> 4% of each run, Pallas kernels for 0% -> 0%
where the time goes in v1:
time: 375 us
  waiting for transfers between devices  237 us (63%)
  matrix products  45.3 us (12%)
  blocking collectives  35.3 us (9%)
  local copies, waits for them, and re-layouts  27 us (7%)
  between operations  15.6 us (4%)
  starting transfers between devices  14.5 us (4%)
    psum x4, waiting for transfers between devices, shards(): moments = lax.psum(lax.psum(moments, ('row', 'col')), 'freq')  227 us
    psum x1, blocking collectives, shards(): lax.psum(jnp.sum(smoothed, axis=(1, 2), dtype=jnp.float32), ('row', 'col'))  30.9 us
    dot_general x1, matrix products, shards(): jnp.einsum('cim,cjm->cij', widened, band_cols, preferred_element_type=jnp...  17 us
    ppermute x2, starting transfers between devices, with_halo(): lax.ppermute(tail, axis, [(i, (i + 1) % count) for i in range(ends)])  8 us
  transfers between devices with their start and end apart: 9, of which 6 were waited for; matrix products, arithmetic and copies ran while one was open for 4% of the time, Pallas kernels for 0%

profile of v1, /device:TPU:0, one launch (start us, length us, event | category | flops | bytes accessed | tf_op | source)
XLA Modules:
  0.0 374.6 jit_solution(1506085563751010675)
XLA Ops:
  8.5 5.0 %collective-permute-start = (bf16[256,8,128]{2,1,0:T(8,128)(2,1)S(1)}, bf16[256,8,128]{2,1,0:T(8,128)(2,1)S(1)}, u32[]{:S(2)}, u32[]{:S(2)}) collective-permute-start(bf16[256,8,128]{2,1,0:T(8,128)(2,1)S(1)} %get-tuple-element.4), channel_id=1, source_target_pairs={{0,4},{4,8},{8,12},{1,5},{5,9},{9,13},{2,6},{6,10},{10,14},{3,7},{... | collective-permute-start | bytes 1572872 | tf_op jit(solution)/shard_map/ppermute | solution.py:19
  15.4 3.8 %copy.7 = bf16[256,32,48]{2,1,0:T(8,128)(2,1)} copy(bf16[256,32,48]{0,2,1:T(8,128)(2,1)S(1)} %convolution_convert_fusion.2) | data formatting | bytes 1572864 | tf_op jit(solution)/shard_map/convert_element_type | solution.py:40
  19.2 5.4 %collective-permute-done = bf16[256,8,128]{2,1,0:T(8,128)(2,1)S(1)} collective-permute-done((bf16[256,8,128]{2,1,0:T(8,128)(2,1)S(1)}, bf16[256,8,128]{2,1,0:T(8,128)(2,1)S(1)}, u32[]{:S(2)}, u32[]{:S(2)}) %collective-permute-start) | collective-permute-done | bytes 524320 | tf_op jit(solution)/shard_map/ppermute | solution.py:19
  24.6 4.3 %collective-permute-done.1 = bf16[256,8,128]{2,1,0:T(8,128)(2,1)} collective-permute-done((bf16[256,8,128]{2,1,0:T(8,128)(2,1)S(1)}, bf16[256,8,128]{2,1,0:T(8,128)(2,1)}, u32[]{:S(2)}, u32[]{:S(2)}) %collective-permute-start.1) | collective-permute-done | bytes 524320 | tf_op jit(solution)/shard_map/ppermute | solution.py:21
  28.9 3.3 fusion.13
  32.2 2.9 fusion.75
  35.1 2.7 copy.8
  37.8 2.7 copy.9
  41.8 3.0 collective-permute-start.2
  44.9 5.2 %convolution_convert_fusion = bf16[256,128,144]{1,0,2:T(8,128)(2,1)} fusion(s32[128,144]{0,1:T(8,128)S(1)} %iota_subtract_fusion, f32[256]{0:T(256)S(1)} %fusion.55, f32[256]{0:T(256)S(1)} %multiply_multiply_fusion.2, f32[17]{0:T(128)S(1)} %multiply_negate_fusion), kind=kOutput, calls=%fused_computation.2 | convolution fusion | flops 165477120 | bytes 9513028 | tf_op jit(solution)/shard_map/ijk,ck->cij/dot_general | solution.py:40
  50.1 3.7 copy.10
  53.8 3.7 copy.11
  57.5 17.0 %convert_reduce_fusion = (f32[256]{0:T(256)S(1)}, bf16[256,32,128]{2,1,0:T(8,128)(2,1)}) fusion(bf16[256,128,144]{1,0,2:T(8,128)(2,1)} %convolution_convert_fusion, bf16[256,32,8]{2,1,0:T(8,128)(2,1)} %copy.11, bf16[256,32,128]{2,1,0:T(8,128)(2,1)S(1)} %fusion.13, bf16[256,32,8]{2,1,0:T(8,128)(2,1)} %copy.10), kind=kOutput, calls=%fused_computation.9 | convolution fusion | flops 312213248 | bytes 13894656 | tf_op jit(solution)/shard_map/cim,cjm->cij/dot_general | solution.py:75
  74.4 2.5 all_to_all.14
  77.0 2.2 copy.13
  79.2 3.8 %all-to-all-start = ((bf16[256,2,2048]{2,0,1:T(8,128)(2,1)}), bf16[256,2,2048]{2,0,1:T(8,128)(2,1)S(1)}, u32[]{:S(2)}, u32[]{:S(2)}) async-start(bf16[256,2,2048]{2,0,1:T(8,128)(2,1)} %copy.13), calls=%async_computation | async-start | bytes 4194304 | tf_op jit(solution)/shard_map/all_to_all | solution.py:80
  83.0 30.9 %psum.35 = f32[256]{0:T(256)S(1)} all-reduce(f32[256]{0:T(256)S(1)} %get-tuple-element.6), channel_id=1, replica_groups=mesh['freq'=2,'row'=4,'col'=4] {'row','col'}, use_global_device_ids=true, to_apply=%region_2.0 | all-reduce | flops 256 | bytes 2048 | tf_op jit(solution)/shard_map/psum | solution.py:78
  113.9 4.5 %all-gather = f32[2,1,256]{2,1,0:T(1,128)S(1)} all-gather(f32[1,1,256]{2,1,0:T(1,128)S(1)} %bitcast.82), channel_id=1, replica_groups=mesh['freq'=2,'row'=4,'col'=4] {'freq'}, dimensions={0}, use_global_device_ids=true | all-gather | bytes 3072 | tf_op jit(solution)/shard_map/all_gather | solution.py:83
  120.2 2.9 subtract_convert_fusion
  125.1 86.3 %all-reduce.5.cloned.1.call-done = f32[128,512]{1,0:T(8,128)} async-done(((f32[128,512]{1,0:T(8,128)}), f32[128,512]{1,0:T(8,128)}) %all-reduce.5.cloned.1.call-update) | async-done | bytes 262160 | tf_op jit(solution)/shard_map/psum | solution.py:92
  211.5 25.9 %all-reduce.7.cloned.1.call-done = f32[128,512]{1,0:T(8,128)} async-done(((f32[128,512]{1,0:T(8,128)}), f32[128,512]{1,0:T(8,128)}) %all-reduce.7.cloned.1.call-update) | async-done | bytes 262160 | tf_op jit(solution)/shard_map/psum | solution.py:92
  245.4 88.8 %all-reduce.9.cloned.1.call-done = f32[128,512]{1,0:T(8,128)} async-done(((f32[128,512]{1,0:T(8,128)}), f32[128,512]{1,0:T(8,128)}) %all-reduce.9.cloned.1.call-update) | async-done | bytes 262160 | tf_op jit(solution)/shard_map/psum | solution.py:92
  334.3 25.9 %all-reduce.11.cloned.1.call-done = f32[128,512]{1,0:T(8,128)} async-done(((f32[128,512]{1,0:T(8,128)}), f32[128,512]{1,0:T(8,128)}) %all-reduce.11.cloned.1.call-update) | async-done | bytes 262160 | tf_op jit(solution)/shard_map/psum | solution.py:92
  360.2 2.1 multiply_reduce_fusion
  (70 shorter events, 20.4 us)
Async XLA Ops:
  7.2 111.2 %copy-start = (bf16[512,512]{1,0:T(8,128)(2,1)S(1)}, bf16[512,512]{1,0:T(8,128)(2,1)}, u32[]{:S(2)}) copy-start(bf16[512,512]{1,0:T(8,128)(2,1)} %param.6) | copy-start | bytes 1572868
  7.2 7.6 %copy-start.6 = (f32[256]{0:T(256)S(1)}, f32[256]{0:T(256)}, u32[]{:S(2)}) copy-start(f32[256]{0:T(256)} %param.5) | copy-start | bytes 3076
  8.5 16.1 %collective-permute-start = (bf16[256,8,128]{2,1,0:T(8,128)(2,1)S(1)}, bf16[256,8,128]{2,1,0:T(8,128)(2,1)S(1)}, u32[]{:S(2)}, u32[]{:S(2)}) collective-permute-start(bf16[256,8,128]{2,1,0:T(8,128)(2,1)S(1)} %get-tuple-element.4), channel_id=1, source_target_pairs={{0,4},{4,8},{8,12},{1,5},{5,9},{9,13},{2,6},{6,10},{10,14},{3,7},{... | collective-permute-start | bytes 1572872 | tf_op jit(solution)/shard_map/ppermute | solution.py:19
  13.5 15.4 %collective-permute-start.1 = (bf16[256,8,128]{2,1,0:T(8,128)(2,1)S(1)}, bf16[256,8,128]{2,1,0:T(8,128)(2,1)}, u32[]{:S(2)}, u32[]{:S(2)}) collective-permute-start(bf16[256,8,128]{2,1,0:T(8,128)(2,1)S(1)} %get-tuple-element.5), channel_id=1, source_target_pairs={{4,0},{8,4},{12,8},{5,1},{9,5},{13,9},{6,2},{10,6},{14,10},{7,3},{... | collective-permute-start | bytes 1572872 | tf_op jit(solution)/shard_map/ppermute | solution.py:21
  40.5 13.3 %collective-permute-start.3 = (bf16[256,32,8]{0,2,1:T(8,128)(2,1)S(1)}, bf16[256,32,8]{0,2,1:T(8,128)(2,1)S(1)}, u32[]{:S(2)}, u32[]{:S(2)}) collective-permute-start(bf16[256,32,8]{0,2,1:T(8,128)(2,1)S(1)} %copy.9), channel_id=1, source_target_pairs={{1,0},{2,1},{3,2},{5,4},{6,5},{7,6},{9,8},{10,9},{11,10},{13,12},{... | collective-permute-start | bytes 393224 | tf_op jit(solution)/shard_map/ppermute | solution.py:21
  41.8 8.2 %collective-permute-start.2 = (bf16[256,32,8]{0,2,1:T(8,128)(2,1)S(1)}, bf16[256,32,8]{0,2,1:T(8,128)(2,1)S(1)}, u32[]{:S(2)}, u32[]{:S(2)}) collective-permute-start(bf16[256,32,8]{0,2,1:T(8,128)(2,1)S(1)} %copy.8), channel_id=1, source_target_pairs={{0,1},{1,2},{2,3},{4,5},{5,6},{6,7},{8,9},{9,10},{10,11},{12,13},{... | collective-permute-start | bytes 393224 | tf_op jit(solution)/shard_map/ppermute | solution.py:19
  79.2 39.6 %all-to-all-start = ((bf16[256,2,2048]{2,0,1:T(8,128)(2,1)}), bf16[256,2,2048]{2,0,1:T(8,128)(2,1)S(1)}, u32[]{:S(2)}, u32[]{:S(2)}) async-start(bf16[256,2,2048]{2,0,1:T(8,128)(2,1)} %copy.13), calls=%async_computation | async-start | bytes 4194304 | tf_op jit(solution)/shard_map/all_to_all | solution.py:80
  83.0 128.4 %all-reduce.5.cloned.1.call-start = ((), (), s32[]{:S(2)}) async-start(), calls=%async_computation.1 | async-start | bytes 524288 | tf_op jit(solution)/shard_map/psum | solution.py:92
  118.8 1.4 copy-start.2
  120.2 3.0 copy-start.1
  125.1 112.3 %all-reduce.7.cloned.1.call-start = ((), (), s32[]{:S(2)}) async-start(), calls=%async_computation.2 | async-start | bytes 524288 | tf_op jit(solution)/shard_map/psum | solution.py:92
  211.4 122.8 %all-reduce.9.cloned.1.call-start = ((), (), s32[]{:S(2)}) async-start(), calls=%async_computation.3 | async-start | bytes 524288 | tf_op jit(solution)/shard_map/psum | solution.py:92
  237.4 5.8 %copy-start.3 = (f32[128,512]{1,0:T(8,128)S(1)}, f32[128,512]{1,0:T(8,128)}, u32[]{:S(2)}) copy-start(f32[128,512]{1,0:T(8,128)} %all-reduce.7.cloned.1.call-done) | copy-start | bytes 786436
  245.4 114.8 %all-reduce.11.cloned.1.call-start = ((), (), s32[]{:S(2)}) async-start(), calls=%async_computation.4 | async-start | bytes 524288 | tf_op jit(solution)/shard_map/psum | solution.py:92
  360.2 5.8 %copy-start.4 = (f32[128,512]{1,0:T(8,128)S(1)}, f32[128,512]{1,0:T(8,128)}, u32[]{:S(2)}) copy-start(f32[128,512]{1,0:T(8,128)} %all-reduce.11.cloned.1.call-done) | copy-start | bytes 786436
  366.4 1.6 copy-start.5
Sparse Core Ops, SparseCore 0:
  125.2 86.1 all-reduce.4
  213.7 23.6 all-reduce.6
  245.5 88.7 all-reduce.8
  336.5 23.6 all-reduce.10
